TPU v7x, 512 devices: a whole 4x4x16 slice. The times are simulated.
512 devices in a mesh: row: 64 (over x, z), col: 8 (over y, core).
Axes of the slice: x: 4, y: 4, z: 16, core: 2. Of those that a mesh axis runs over, the one named last changes fastest.
Arguments:
- current: bfloat16 [2, 256, 32, 4, 128], P(None, 'row', 'col'), may hold values from -6 to 6
- probe: bfloat16 [2, 256, 32, 4, 128], P(None, 'row', 'col'), may hold values from -6 to 6
- near_list: int32 [256, 32, 2], P('row', 'col'), may hold values from 0 to 9, as said below
- near_blocks: bfloat16 [2, 256, 32, 2, 128, 128], P(None, 'row', 'col'), may hold values from -0.25 to 0.25
- radiation: bfloat16 [2, 128, 128], replicated, may hold values from -0.375 to 0.375
- reception: bfloat16 [2, 128, 128], replicated, may hold values from -0.375 to 0.375
- interp: float32 [256, 128], replicated, may hold values from -0.5 to 0.5
- phase: float32 [16, 256], replicated, may hold values from -3.140625 to 3.140625
- leaf_table: float32 [2, 15, 15, 128], replicated, may hold values from -0.36 to 0.36
- coarse_table: bfloat16 [2, 127, 15, 256], replicated, may hold values from -0.023925781 to 0.023925781
Outputs:
- forward_out: float32 [2, 256, 32, 4, 128], P(None, 'row', 'col')
- adjoint_out: float32 [2, 256, 32, 4, 128], P(None, 'row', 'col')
Inputs may be any that keep to these rules, and one draw needn't show every extreme that they name: `near_list`: the 2 slots of a box hold distinct codes; only slots after the first may be empty (code 9).
All inputs are finite; a program needn't handle non-finite values.
Results may differ from a plain program's by a relative error of at most 0.0027.
Values may be sent and summed in bfloat16 or wider, within the bound.
No kernel may reach another device: no remote copies, remote signals or barrier semaphores. Data moves between devices by JAX's collectives and lax.ppermute only.
A program may use at most 128 MiB of HBM per device.

v0:
```python
import jax
import jax.numpy as jnp
from jax import lax
from jax.sharding import PartitionSpec as P

HIGH = lax.Precision.HIGHEST


def with_halo(cells, sides, width):
    for axis, dim in sides:
        count = lax.axis_size(axis)
        ends = count - 1
        head = lax.slice_in_dim(cells, 0, width, axis=dim)
        tail = lax.slice_in_dim(cells, cells.shape[dim] - width, cells.shape[dim], axis=dim)
        cells = jnp.concatenate(
            [
                lax.ppermute(tail, axis, [(i, (i + 1) % count) for i in range(ends)]),
                cells,
                lax.ppermute(head, axis, [((i + 1) % count, i) for i in range(ends)]),
            ],
            axis=dim,
        )
    return cells


def from_behind(block, axis, distance):
    devices = range(lax.axis_size(axis))
    route = [(i - distance, i) for i in devices if i - distance in devices]
    return lax.ppermute(block, axis, route)


def complex_mul(left_re, left_im, right_re, right_im):
    return (left_re * right_re - left_im * right_im, left_re * right_im + left_im * right_re)


def conj_flip(table, axes):
    flipped = jnp.flip(table, axes)
    return jnp.stack([flipped[0], -flipped[1]])


def product(form, left, right):
    return jnp.einsum(form, left, right, preferred_element_type=jnp.float32)


def near_field(current, probe, near_list, near_blocks):
    box_side = current.shape[1]
    one_hot = (near_list[..., None] == jnp.arange(9)).astype(jnp.bfloat16)
    blocks_re = near_blocks[0]
    blocks_im = near_blocks[1]
    padded = with_halo(current, (("row", 1), ("col", 2)), 1)
    shifted = jnp.stack(
        [
            padded[
                :,
                offset_code // 3 : offset_code // 3 + box_side,
                offset_code % 3 : offset_code % 3 + box_side,
            ]
            for offset_code in range(9)
        ]
    )
    picked = product("rcko,oxrcmp->xkrcmp", one_hot, shifted).astype(jnp.bfloat16)
    fwd_re = product("rckpq,krcmq->rcmp", blocks_re, picked[0]) - product(
        "rckpq,krcmq->rcmp", blocks_im, picked[1]
    )
    fwd_im = product("rckpq,krcmq->rcmp", blocks_re, picked[1]) + product(
        "rckpq,krcmq->rcmp", blocks_im, picked[0]
    )
    near_fwd = jnp.stack([fwd_re, fwd_im])
    back_re = product("rckpq,rcmp->krcmq", blocks_re, probe[0]) + product(
        "rckpq,rcmp->krcmq", blocks_im, probe[1]
    )
    back_im = product("rckpq,rcmp->krcmq", blocks_re, probe[1]) - product(
        "rckpq,rcmp->krcmq", blocks_im, probe[0]
    )
    contrib = jnp.stack([back_re, back_im])
    placed_all = jnp.einsum(
        "rcko,xkrcmp->oxrcmp", one_hot.astype(jnp.float32), contrib, precision=HIGH
    )
    placed = jnp.zeros((2, box_side + 2, box_side + 2) + contrib.shape[4:], jnp.float32)
    for offset_code in range(9):
        placed = placed.at[
            :,
            offset_code // 3 : offset_code // 3 + box_side,
            offset_code % 3 : offset_code % 3 + box_side,
        ].add(placed_all[offset_code])
    for step_dir, send_row, keep_row in ((1, box_side + 1, 1), (-1, 0, box_side)):
        arrived = from_behind(placed[:, send_row], "row", step_dir)
        placed = placed.at[:, keep_row].add(arrived)
    for step_dir, send_col, keep_col in ((1, box_side + 1, 1), (-1, 0, box_side)):
        arrived = from_behind(placed[:, 1 : box_side + 1, send_col], "col", step_dir)
        placed = placed.at[:, 1 : box_side + 1, keep_col].add(arrived)
    return (near_fwd, placed[:, 1 : box_side + 1, 1 : box_side + 1])


def far_field(vectors, rad_tab, rcv_tab, leaf_tab, coarse_tab, interp, phase):
    box_side = vectors.shape[2]
    span = 3 * box_side
    reach = 2 * box_side - 1
    out_re = product("srcmp,sqp->srcmq", vectors[:, 0], rad_tab[:, 0]) - product(
        "srcmp,sqp->srcmq", vectors[:, 1], rad_tab[:, 1]
    )
    out_im = product("srcmp,sqp->srcmq", vectors[:, 0], rad_tab[:, 1]) + product(
        "srcmp,sqp->srcmq", vectors[:, 1], rad_tab[:, 0]
    )
    leaf_out = jnp.stack([out_re, out_im], 1)
    window = with_halo(leaf_out, (("row", 2), ("col", 3)), box_side)
    offsets = jnp.arange(2 * reach + 1) - reach
    near_offset = jnp.abs(offsets) <= 1
    keep = 1.0 - (near_offset[:, None] & near_offset[None, :]).astype(jnp.float32)
    masked = leaf_tab * keep[None, None, :, :, None]
    rows_in = []
    for row_pos in range(box_side):
        cols_in = []
        for col_pos in range(box_side):
            row_first = box_side - 1 - row_pos
            col_first = box_side - 1 - col_pos
            coeffs = masked[:, :, row_first : row_first + span, col_first : col_first + span]
            part_re, part_im = complex_mul(
                coeffs[:, 0, :, :, None], coeffs[:, 1, :, :, None], window[:, 0], window[:, 1]
            )
            cols_in.append(jnp.stack([part_re.sum((1, 2)), part_im.sum((1, 2))], 1))
        rows_in.append(jnp.stack(cols_in, 2))
    leaf_in = jnp.stack(rows_in, 2)
    interpolated = jnp.einsum("kq,sxrcmq->sxrcmk", interp, leaf_out, precision=HIGH)
    angles = phase.reshape(box_side, box_side, -1)
    cos_ph = jnp.cos(angles)[:, :, None, :]
    sin_ph = jnp.sin(angles)[:, :, None, :]
    top_re = (cos_ph * interpolated[:, 0] - sin_ph * interpolated[:, 1]).sum((1, 2))
    top_im = (cos_ph * interpolated[:, 1] + sin_ph * interpolated[:, 0]).sum((1, 2))
    top_b = jnp.stack([top_re, top_im], 1).astype(jnp.bfloat16)
    row_idx = lax.axis_index("row")
    col_idx = lax.axis_index("col")
    row_count = lax.axis_size("row")
    col_count = lax.axis_size("col")
    flat_tab = coarse_tab.reshape(
        coarse_tab.shape[0], 2, coarse_tab.shape[2] * coarse_tab.shape[3], coarse_tab.shape[4]
    )
    portion = lax.all_gather(top_b[:, :, None], ("row", "col"), axis=2, tiled=True)
    sources = jnp.arange(portion.shape[2])
    src_rows = sources // col_count
    src_cols = sources % col_count
    flat_index = (row_idx - src_rows + row_count - 1) * (2 * col_count - 1) + (
        col_idx - src_cols + col_count - 1
    )
    coeff = jnp.take(flat_tab, flat_index, axis=2).astype(jnp.float32)
    distant = ((jnp.abs(row_idx - src_rows) > 1) | (jnp.abs(col_idx - src_cols) > 1)).astype(
        jnp.float32
    )
    coef_re = coeff[:, 0] * distant[None, :, None]
    coef_im = coeff[:, 1] * distant[None, :, None]
    values = portion.astype(jnp.float32)
    got_re = jnp.einsum("snq,snmq->smq", coef_re, values[:, 0], precision=HIGH) - jnp.einsum(
        "snq,snmq->smq", coef_im, values[:, 1], precision=HIGH
    )
    got_im = jnp.einsum("snq,snmq->smq", coef_re, values[:, 1], precision=HIGH) + jnp.einsum(
        "snq,snmq->smq", coef_im, values[:, 0], precision=HIGH
    )
    coarse_in = jnp.stack([got_re, got_im], 1)
    in_re = coarse_in[:, 0][:, None, None]
    in_im = coarse_in[:, 1][:, None, None]
    back_re = cos_ph * in_re + sin_ph * in_im
    back_im = cos_ph * in_im - sin_ph * in_re
    spread = jnp.einsum(
        "kq,sxrcmk->sxrcmq", interp, jnp.stack([back_re, back_im], 1), precision=HIGH
    )
    incoming = (leaf_in + spread).astype(jnp.bfloat16)
    res_re = product("srcmq,spq->srcmp", incoming[:, 0], rcv_tab[:, 0]) - product(
        "srcmq,spq->srcmp", incoming[:, 1], rcv_tab[:, 1]
    )
    res_im = product("srcmq,spq->srcmp", incoming[:, 0], rcv_tab[:, 1]) + product(
        "srcmq,spq->srcmp", incoming[:, 1], rcv_tab[:, 0]
    )
    return jnp.stack([res_re, res_im], 1)


def per_device(
    current,
    probe,
    near_list,
    near_blocks,
    radiation,
    reception,
    interp,
    phase,
    leaf_table,
    coarse_table,
):
    near_fwd, near_adj = near_field(current, probe, near_list, near_blocks)
    fwd_set = (radiation, reception, leaf_table, coarse_table)
    adj_set = (
        jnp.stack([reception[0].T, -reception[1].T]),
        jnp.stack([radiation[0].T, -radiation[1].T]),
        conj_flip(leaf_table, (1, 2)),
        conj_flip(coarse_table, (1, 2)),
    )
    far_fwd = far_field(
        current[None],
        fwd_set[0][None],
        fwd_set[1][None],
        fwd_set[2][None],
        fwd_set[3][None],
        interp,
        phase,
    )[0]
    far_adj = far_field(
        probe[None],
        adj_set[0][None],
        adj_set[1][None],
        adj_set[2][None],
        adj_set[3][None],
        interp,
        phase,
    )[0]
    return (near_fwd + far_fwd, near_adj + far_adj)


def solution(mesh):
    placed = (
        P(None, "row", "col", None, None),
        P(None, "row", "col", None, None),
        P("row", "col", None),
        P(None, "row", "col", None, None, None),
        P(),
        P(),
        P(),
        P(),
        P(),
        P(),
    )
    return jax.shard_map(
        per_device,
        mesh=mesh,
        in_specs=placed,
        out_specs=(P(None, "row", "col", None, None), P(None, "row", "col", None, None)),
        check_vma=False,
    )
```

profile of v0, /device:TPU:1, one launch (start us, length us, event | category | flops | bytes accessed | tf_op | source)
XLA Modules:
  0.0 378.0 jit_solution(1067463419828961562)
XLA Ops:
  19.8 5.6 %collective-permute-start.4 = (f32[1,2,4,4,4,128]{5,4,3,2,1,0:T(4,128)}, f32[1,2,4,4,4,128]{5,4,3,2,1,0:T(4,128)}, u32[]{:S(2)}, u32[]{:S(2)}) collective-permute-start(f32[1,2,4,4,4,128]{5,4,3,2,1,0:T(4,128)} %pad_maximum_fusion.5), channel_id=1, source_target_pairs={{0,8},{8,16},{16,24},{24,32},{32,40},{40,48},{48,56},{56,64},{64,7... | collective-permute-start | bytes 196616 | tf_op jit(solution)/shard_map/ppermute | solution.py:17
  27.3 4.6 %collective-permute-start = (bf16[2,1,4,4,128]{4,3,2,1,0:T(4,128)(2,1)}, bf16[2,1,4,4,128]{4,3,2,1,0:T(4,128)(2,1)}, u32[]{:S(2)}, u32[]{:S(2)}) collective-permute-start(bf16[2,1,4,4,128]{4,3,2,1,0:T(4,128)(2,1)} %get-tuple-element.431), channel_id=1, source_target_pairs={{0,8},{8,16},{16,24},{24,32},{32,40},{40,48},{48,56},{56,64},{64,7... | collective-permute-start | bytes 24584 | tf_op jit(solution)/shard_map/ppermute | solution.py:17
  35.5 1.9 fusion.131
  42.6 1.6 fusion.128
  45.5 6.5 %fusion.125 = (bf16[1,127,15,256]{3,0,2,1:T(2,128)(2,1)}, bf16[1,127,15,256]{3,0,2,1:T(2,128)(2,1)S(1)}) fusion(bf16[2,127,15,256]{3,0,2,1:T(2,128)(2,1)} %param.47), kind=kLoop, calls=%fused_computation.445 | loop fusion | bytes 3901440 | tf_op jit(solution)/shard_map/slice | solution.py:38
  52.0 3.3 reverse_negate_fusion
  55.3 4.8 %slice.1246 = bf16[1,127,15,256]{3,0,2,1:T(2,128)(2,1)} reverse(bf16[1,127,15,256]{3,0,2,1:T(2,128)(2,1)} %get-tuple-element.295), dimensions={1,2} | reverse | bytes 1950720 | tf_op jit(solution)/shard_map/slice | solution.py:38
  60.1 6.5 %maximum_bitcast_fusion = bf16[2,1905,256]{2,0,1:T(2,128)(2,1)} fusion(bf16[1,1,1905,256]{3,1,2,0:T(2,128)(2,1)} %bitcast.1058, bf16[1,1,1905,256]{3,1,2,0:T(2,128)(2,1)} %bitcast.1059), kind=kLoop, calls=%fused_computation.18 | loop fusion | flops 3901440 | bytes 3901440 | tf_op jit(solution)/shard_map/jit(_take)/Arg_0.13 | solution.py:145
  66.7 4.3 %gather_fusion.1 = bf16[512,2,256]{2,1,0:T(2,128)(2,1)} fusion(bf16[2,1905,256]{2,0,1:T(2,128)(2,1)} %maximum_bitcast_fusion, s32[1024]{0:T(1024)S(1)} %pad_clamp_fusion), kind=kCustom, calls=%fused_computation.1.clone | custom fusion | bytes 1050624 | tf_op jit(solution)/shard_map/jit(_take)/gather | solution.py:145
  70.9 4.3 %gather_fusion = bf16[512,2,256]{2,1,0:T(2,128)(2,1)} fusion(bf16[2,1905,256]{2,0,1:T(2,128)(2,1)} %bitcast.1057, s32[1024]{0:T(1024)S(1)} %pad_clamp_fusion), kind=kCustom, calls=%fused_computation.clone | custom fusion | bytes 1050624 | tf_op jit(solution)/shard_map/jit(_take)/gather | solution.py:145
  76.5 3.3 fusion.45
  79.8 1.8 fusion.127
  88.3 1.6 copy_bitcast_fusion.45
  90.0 1.6 copy_bitcast_fusion.43
  91.6 1.6 copy_bitcast_fusion.41
  93.2 1.7 copy_bitcast_fusion.33
  94.9 1.6 copy_bitcast_fusion.51
  96.6 1.7 copy_bitcast_fusion.49
  107.5 1.9 fusion.63
  109.7 1.6 fusion.49
  115.1 8.9 %collective-permute-start.3 = (bf16[2,6,1,4,128]{4,3,2,1,0:T(4,128)(2,1)S(1)}, bf16[2,6,1,4,128]{4,3,2,1,0:T(4,128)(2,1)S(1)}, u32[]{:S(2)}, u32[]{:S(2)}) collective-permute-start(bf16[2,6,1,4,128]{4,3,2,1,0:T(4,128)(2,1)S(1)} %get-tuple-element.419), channel_id=1, source_target_pairs={{1,0},{2,1},{3,2},{4,3},{5,4},{6,5},{7,6},{9,8},{10,9},{11,10},{12... | collective-permute-start | bytes 36872 | tf_op jit(solution)/shard_map/ppermute | solution.py:19
  124.0 1.9 collective-permute-start.2
  128.2 1.6 copy.524
  129.7 1.6 copy.525
  131.3 1.6 copy.522
  132.9 1.6 copy.523
  134.4 1.6 copy.520
  136.0 1.6 copy.521
  137.5 1.6 copy.512
  139.1 1.6 copy.513
  140.7 1.5 copy.530
  142.2 1.5 copy.531
  150.2 1.5 copy.542
  151.7 1.5 copy.543
  159.8 4.9 %collective-permute-start.12 = (f32[1,2,4,4,4,128]{5,4,3,2,1,0:T(4,128)}, f32[1,2,4,4,4,128]{5,4,3,2,1,0:T(4,128)}, u32[]{:S(2)}, u32[]{:S(2)}) collective-permute-start(f32[1,2,4,4,4,128]{5,4,3,2,1,0:T(4,128)} %pad_maximum_fusion.6), channel_id=1, source_target_pairs={{0,8},{8,16},{16,24},{24,32},{32,40},{40,48},{48,56},{56,64},{64,7... | collective-permute-start | bytes 196616 | tf_op jit(solution)/shard_map/ppermute | solution.py:17
  164.7 1.9 collective-permute-start.8
  168.3 2.5 stack.593
  176.8 2.2 collective-permute-done.9
  179.0 2.3 collective-permute-start.10
  182.2 2.8 collective-permute-start.7
  185.1 2.7 collective-permute-start.6
  187.8 1.9 collective-permute-start.11
  190.7 1.9 collective-permute-start.15
  192.6 3.9 %collective-permute-start.14 = (f32[1,2,12,4,4,128]{5,4,3,2,1,0:T(4,128)S(1)}, f32[1,2,12,4,4,128]{5,4,3,2,1,0:T(4,128)S(1)}, u32[]{:S(2)}, u32[]{:S(2)}) collective-permute-start(f32[1,2,12,4,4,128]{5,4,3,2,1,0:T(4,128)S(1)} %pad_maximum_fusion.3), channel_id=1, source_target_pairs={{0,1},{1,2},{2,3},{3,4},{4,5},{5,6},{6,7},{8,9},{9,10},{10,11},{11... | collective-permute-start | bytes 589832 | tf_op jit(solution)/shard_map/ppermute | solution.py:17
  203.1 1.8 subtract_reduce_fusion.6
  207.9 3.2 fusion.6
  211.2 153.4 %all-gather.3.cloned.1.call-done = bf16[1,2,512,4,256]{4,3,2,1,0:T(4,128)(2,1)} async-done(((bf16[1,2,1,4,256]{4,3,2,1,0:T(4,128)(2,1)}), bf16[1,2,512,4,256]{4,3,2,1,0:T(4,128)(2,1)}) %all-gather.3.cloned.1.call-update) | async-done | bytes 2097168 | tf_op jit(solution)/shard_map/all_gather | solution.py:138
  364.6 3.2 fusion.2
  (489 shorter events, 81.8 us)
Async XLA Ops:
  7.2 27.9 %copy-start.8 = (f32[2,15,15,128]{3,0,2,1:T(2,128)S(1)}, f32[2,15,15,128]{3,0,2,1:T(2,128)}, u32[]{:S(2)}) copy-start(f32[2,15,15,128]{3,0,2,1:T(2,128)} %param.46) | copy-start | bytes 691204
  7.2 200.7 %all-gather.5.cloned.1.call-start = ((), (), s32[]{:S(2)}) async-start(), calls=%async_computation.1 | async-start | bytes 2101248 | tf_op jit(solution)/shard_map/all_gather | solution.py:138
  17.8 346.8 %all-gather.3.cloned.1.call-start = ((), (), s32[]{:S(2)}) async-start(), calls=%async_computation | async-start | bytes 2101248 | tf_op jit(solution)/shard_map/all_gather | solution.py:138
  18.5 162.8 %collective-permute-start.5 = (f32[1,2,4,4,4,128]{5,4,3,2,1,0:T(4,128)}, f32[1,2,4,4,4,128]{5,4,3,2,1,0:T(4,128)}, u32[]{:S(2)}, u32[]{:S(2)}) collective-permute-start(f32[1,2,4,4,4,128]{5,4,3,2,1,0:T(4,128)} %pad_maximum_fusion.5), channel_id=1, source_target_pairs={{8,0},{16,8},{24,16},{32,24},{40,32},{48,40},{56,48},{64,56},{72,6... | collective-permute-start | bytes 196616 | tf_op jit(solution)/shard_map/ppermute | solution.py:19
  19.8 161.5 %collective-permute-start.4 = (f32[1,2,4,4,4,128]{5,4,3,2,1,0:T(4,128)}, f32[1,2,4,4,4,128]{5,4,3,2,1,0:T(4,128)}, u32[]{:S(2)}, u32[]{:S(2)}) collective-permute-start(f32[1,2,4,4,4,128]{5,4,3,2,1,0:T(4,128)} %pad_maximum_fusion.5), channel_id=1, source_target_pairs={{0,8},{8,16},{16,24},{24,32},{32,40},{40,48},{48,56},{56,64},{64,7... | collective-permute-start | bytes 196616 | tf_op jit(solution)/shard_map/ppermute | solution.py:17
  26.0 87.4 %collective-permute-start.1 = (bf16[2,1,4,4,128]{4,3,2,1,0:T(4,128)(2,1)}, bf16[2,1,4,4,128]{4,3,2,1,0:T(4,128)(2,1)}, u32[]{:S(2)}, u32[]{:S(2)}) collective-permute-start(bf16[2,1,4,4,128]{4,3,2,1,0:T(4,128)(2,1)} %get-tuple-element.430), channel_id=1, source_target_pairs={{8,0},{16,8},{24,16},{32,24},{40,32},{48,40},{56,48},{64,56},{72,6... | collective-permute-start | bytes 24584 | tf_op jit(solution)/shard_map/ppermute | solution.py:19
  27.3 85.4 %collective-permute-start = (bf16[2,1,4,4,128]{4,3,2,1,0:T(4,128)(2,1)}, bf16[2,1,4,4,128]{4,3,2,1,0:T(4,128)(2,1)}, u32[]{:S(2)}, u32[]{:S(2)}) collective-permute-start(bf16[2,1,4,4,128]{4,3,2,1,0:T(4,128)(2,1)} %get-tuple-element.431), channel_id=1, source_target_pairs={{0,8},{8,16},{16,24},{24,32},{32,40},{40,48},{48,56},{56,64},{64,7... | collective-permute-start | bytes 24584 | tf_op jit(solution)/shard_map/ppermute | solution.py:17
  32.5 157.2 %collective-permute-start.13 = (f32[1,2,4,4,4,128]{5,4,3,2,1,0:T(4,128)}, f32[1,2,4,4,4,128]{5,4,3,2,1,0:T(4,128)}, u32[]{:S(2)}, u32[]{:S(2)}) collective-permute-start(f32[1,2,4,4,4,128]{5,4,3,2,1,0:T(4,128)} %pad_maximum_fusion.6), channel_id=1, source_target_pairs={{8,0},{16,8},{24,16},{32,24},{40,32},{48,40},{56,48},{64,56},{72,6... | collective-permute-start | bytes 196616 | tf_op jit(solution)/shard_map/ppermute | solution.py:19
  45.5 36.6 %copy-start.132 = (s32[4,4,2]{2,1,0:T(4,128)}, s32[4,4,2]{2,1,0:T(4,128)S(1)}, u32[]{:S(2)}) copy-start(s32[4,4,2]{2,1,0:T(4,128)S(1)} %copy.258) | copy-start | bytes 388
  111.2 32.5 %copy-start.84 = (f32[1,1,12,12,128]{4,0,3,2,1:T(1,128)S(1)}, f32[1,1,12,12,128]{4,0,3,2,1:T(1,128)}, u32[]{:S(2)}) copy-start(f32[1,1,12,12,128]{4,0,3,2,1:T(1,128)} %get-tuple-element.355) | copy-start | bytes 221188
  111.2 33.1 %copy-start.83 = (f32[1,1,12,12,128]{4,0,3,2,1:T(1,128)S(1)}, f32[1,1,12,12,128]{4,0,3,2,1:T(1,128)}, u32[]{:S(2)}) copy-start(f32[1,1,12,12,128]{4,0,3,2,1:T(1,128)} %get-tuple-element.356) | copy-start | bytes 221188
  111.2 33.8 %copy-start.82 = (f32[1,1,12,12,128]{4,0,3,2,1:T(1,128)S(1)}, f32[1,1,12,12,128]{4,0,3,2,1:T(1,128)}, u32[]{:S(2)}) copy-start(f32[1,1,12,12,128]{4,0,3,2,1:T(1,128)} %get-tuple-element.353) | copy-start | bytes 221188
  111.2 34.4 %copy-start.81 = (f32[1,1,12,12,128]{4,0,3,2,1:T(1,128)S(1)}, f32[1,1,12,12,128]{4,0,3,2,1:T(1,128)}, u32[]{:S(2)}) copy-start(f32[1,1,12,12,128]{4,0,3,2,1:T(1,128)} %get-tuple-element.354) | copy-start | bytes 221188
  111.2 35.1 %copy-start.80 = (f32[1,1,12,12,128]{4,0,3,2,1:T(1,128)S(1)}, f32[1,1,12,12,128]{4,0,3,2,1:T(1,128)}, u32[]{:S(2)}) copy-start(f32[1,1,12,12,128]{4,0,3,2,1:T(1,128)} %get-tuple-element.341) | copy-start | bytes 221188
  111.2 35.7 %copy-start.79 = (f32[1,1,12,12,128]{4,0,3,2,1:T(1,128)S(1)}, f32[1,1,12,12,128]{4,0,3,2,1:T(1,128)}, u32[]{:S(2)}) copy-start(f32[1,1,12,12,128]{4,0,3,2,1:T(1,128)} %get-tuple-element.342) | copy-start | bytes 221188
  111.2 36.3 %copy-start.78 = (f32[1,1,12,12,128]{4,0,3,2,1:T(1,128)S(1)}, f32[1,1,12,12,128]{4,0,3,2,1:T(1,128)}, u32[]{:S(2)}) copy-start(f32[1,1,12,12,128]{4,0,3,2,1:T(1,128)} %get-tuple-element.343) | copy-start | bytes 221188
  111.3 37.0 %copy-start.77 = (f32[1,1,12,12,128]{4,0,3,2,1:T(1,128)S(1)}, f32[1,1,12,12,128]{4,0,3,2,1:T(1,128)}, u32[]{:S(2)}) copy-start(f32[1,1,12,12,128]{4,0,3,2,1:T(1,128)} %get-tuple-element.344) | copy-start | bytes 221188
  111.3 37.6 %copy-start.76 = (f32[1,1,12,12,128]{4,0,3,2,1:T(1,128)S(1)}, f32[1,1,12,12,128]{4,0,3,2,1:T(1,128)}, u32[]{:S(2)}) copy-start(f32[1,1,12,12,128]{4,0,3,2,1:T(1,128)} %get-tuple-element.345) | copy-start | bytes 221188
  111.3 38.3 %copy-start.75 = (f32[1,1,12,12,128]{4,0,3,2,1:T(1,128)S(1)}, f32[1,1,12,12,128]{4,0,3,2,1:T(1,128)}, u32[]{:S(2)}) copy-start(f32[1,1,12,12,128]{4,0,3,2,1:T(1,128)} %get-tuple-element.346) | copy-start | bytes 221188
  114.4 38.8 %copy-start.102 = (f32[1,1,12,12,128]{4,0,3,2,1:T(1,128)S(1)}, f32[1,1,12,12,128]{4,0,3,2,1:T(1,128)}, u32[]{:S(2)}) copy-start(f32[1,1,12,12,128]{4,0,3,2,1:T(1,128)} %get-tuple-element.366) | copy-start | bytes 221188
  115.1 44.6 %collective-permute-start.3 = (bf16[2,6,1,4,128]{4,3,2,1,0:T(4,128)(2,1)S(1)}, bf16[2,6,1,4,128]{4,3,2,1,0:T(4,128)(2,1)S(1)}, u32[]{:S(2)}, u32[]{:S(2)}) collective-permute-start(bf16[2,6,1,4,128]{4,3,2,1,0:T(4,128)(2,1)S(1)} %get-tuple-element.419), channel_id=1, source_target_pairs={{1,0},{2,1},{3,2},{4,3},{5,4},{6,5},{7,6},{9,8},{10,9},{11,10},{12... | collective-permute-start | bytes 36872 | tf_op jit(solution)/shard_map/ppermute | solution.py:19
  124.0 40.7 %collective-permute-start.2 = (bf16[2,6,1,4,128]{4,3,2,1,0:T(4,128)(2,1)S(1)}, bf16[2,6,1,4,128]{4,3,2,1,0:T(4,128)(2,1)S(1)}, u32[]{:S(2)}, u32[]{:S(2)}) collective-permute-start(bf16[2,6,1,4,128]{4,3,2,1,0:T(4,128)(2,1)S(1)} %get-tuple-element.420), channel_id=1, source_target_pairs={{0,1},{1,2},{2,3},{3,4},{4,5},{5,6},{6,7},{8,9},{9,10},{10,11},{11... | collective-permute-start | bytes 36872 | tf_op jit(solution)/shard_map/ppermute | solution.py:17
  125.9 27.9 %copy-start.101 = (f32[1,1,12,12,128]{4,0,3,2,1:T(1,128)S(1)}, f32[1,1,12,12,128]{4,0,3,2,1:T(1,128)}, u32[]{:S(2)}) copy-start(f32[1,1,12,12,128]{4,0,3,2,1:T(1,128)} %get-tuple-element.367) | copy-start | bytes 221188
  128.2 26.3 %copy-start.100 = (f32[1,1,12,12,128]{4,0,3,2,1:T(1,128)S(1)}, f32[1,1,12,12,128]{4,0,3,2,1:T(1,128)}, u32[]{:S(2)}) copy-start(f32[1,1,12,12,128]{4,0,3,2,1:T(1,128)} %get-tuple-element.357) | copy-start | bytes 221188
  129.7 25.4 %copy-start.74 = (f32[1,1,12,12,128]{4,0,3,2,1:T(1,128)S(1)}, f32[1,1,12,12,128]{4,0,3,2,1:T(1,128)}, u32[]{:S(2)}) copy-start(f32[1,1,12,12,128]{4,0,3,2,1:T(1,128)} %get-tuple-element.338) | copy-start | bytes 221188
  131.3 24.5 %copy-start.99 = (f32[1,1,12,12,128]{4,0,3,2,1:T(1,128)S(1)}, f32[1,1,12,12,128]{4,0,3,2,1:T(1,128)}, u32[]{:S(2)}) copy-start(f32[1,1,12,12,128]{4,0,3,2,1:T(1,128)} %get-tuple-element.360) | copy-start | bytes 221188
  159.8 30.0 %collective-permute-start.12 = (f32[1,2,4,4,4,128]{5,4,3,2,1,0:T(4,128)}, f32[1,2,4,4,4,128]{5,4,3,2,1,0:T(4,128)}, u32[]{:S(2)}, u32[]{:S(2)}) collective-permute-start(f32[1,2,4,4,4,128]{5,4,3,2,1,0:T(4,128)} %pad_maximum_fusion.6), channel_id=1, source_target_pairs={{0,8},{8,16},{16,24},{24,32},{32,40},{40,48},{48,56},{56,64},{64,7... | collective-permute-start | bytes 196616 | tf_op jit(solution)/shard_map/ppermute | solution.py:17
  164.7 8.9 %collective-permute-start.8 = (f32[2,6,4,128]{3,2,0,1:T(4,128)}, f32[2,6,4,128]{3,2,0,1:T(4,128)}, u32[]{:S(2)}, u32[]{:S(2)}) collective-permute-start(f32[2,6,4,128]{3,2,0,1:T(4,128)} %slice_bitcast_fusion.41), channel_id=1, source_target_pairs={{0,8},{8,16},{16,24},{24,32},{32,40},{40,48},{48,56},{56,64},{64,7... | collective-permute-start | bytes 73736 | tf_op jit(solution)/shard_map/ppermute | solution.py:29
  173.2 24.8 %copy-start.62 = (f32[12,12,128]{2,1,0:T(8,128)S(1)}, f32[12,12,128]{2,1,0:T(8,128)}, u32[]{:S(2)}) copy-start(f32[12,12,128]{2,1,0:T(8,128)} %get-tuple-element.454) | copy-start | bytes 221188
  173.2 24.8 %copy-start.63 = (f32[12,12,128]{2,1,0:T(8,128)S(1)}, f32[12,12,128]{2,1,0:T(8,128)}, u32[]{:S(2)}) copy-start(f32[12,12,128]{2,1,0:T(8,128)} %get-tuple-element.455) | copy-start | bytes 221188
  173.2 24.8 %copy-start.64 = (f32[12,12,128]{2,1,0:T(8,128)S(1)}, f32[12,12,128]{2,1,0:T(8,128)}, u32[]{:S(2)}) copy-start(f32[12,12,128]{2,1,0:T(8,128)} %get-tuple-element.452) | copy-start | bytes 221188
  173.2 24.8 %copy-start.65 = (f32[12,12,128]{2,1,0:T(8,128)S(1)}, f32[12,12,128]{2,1,0:T(8,128)}, u32[]{:S(2)}) copy-start(f32[12,12,128]{2,1,0:T(8,128)} %get-tuple-element.453) | copy-start | bytes 221188
  173.2 24.8 %copy-start.66 = (f32[12,12,128]{2,1,0:T(8,128)S(1)}, f32[12,12,128]{2,1,0:T(8,128)}, u32[]{:S(2)}) copy-start(f32[12,12,128]{2,1,0:T(8,128)} %get-tuple-element.450) | copy-start | bytes 221188
  173.2 24.8 %copy-start.67 = (f32[12,12,128]{2,1,0:T(8,128)S(1)}, f32[12,12,128]{2,1,0:T(8,128)}, u32[]{:S(2)}) copy-start(f32[12,12,128]{2,1,0:T(8,128)} %get-tuple-element.451) | copy-start | bytes 221188
  173.2 24.8 %copy-start.68 = (f32[12,12,128]{2,1,0:T(8,128)S(1)}, f32[12,12,128]{2,1,0:T(8,128)}, u32[]{:S(2)}) copy-start(f32[12,12,128]{2,1,0:T(8,128)} %get-tuple-element.442) | copy-start | bytes 221188
  173.2 24.8 %copy-start.69 = (f32[12,12,128]{2,1,0:T(8,128)S(1)}, f32[12,12,128]{2,1,0:T(8,128)}, u32[]{:S(2)}) copy-start(f32[12,12,128]{2,1,0:T(8,128)} %get-tuple-element.443) | copy-start | bytes 221188
  174.4 4.6 %collective-permute-start.9 = (f32[2,6,4,128]{3,2,0,1:T(4,128)S(1)}, f32[2,6,4,128]{3,2,0,1:T(4,128)S(1)}, u32[]{:S(2)}, u32[]{:S(2)}) collective-permute-start(f32[2,6,4,128]{3,2,0,1:T(4,128)S(1)} %slice_bitcast_fusion.40), channel_id=1, source_target_pairs={{8,0},{16,8},{24,16},{32,24},{40,32},{48,40},{56,48},{64,56},{72,6... | collective-permute-start | bytes 73736 | tf_op jit(solution)/shard_map/ppermute | solution.py:29
  179.0 8.8 %collective-permute-start.10 = (f32[2,4,4,128]{3,2,0,1:T(4,128)S(1)}, f32[2,4,4,128]{3,2,0,1:T(4,128)S(1)}, u32[]{:S(2)}, u32[]{:S(2)}) collective-permute-start(f32[2,4,4,128]{3,2,0,1:T(4,128)S(1)} %slice_bitcast_fusion.47), channel_id=1, source_target_pairs={{0,1},{1,2},{2,3},{3,4},{4,5},{5,6},{6,7},{8,9},{9,10},{10,11},{11... | collective-permute-start | bytes 49160 | tf_op jit(solution)/shard_map/ppermute | solution.py:29
  182.2 14.5 %collective-permute-start.7 = (f32[1,2,12,4,4,128]{5,4,3,2,1,0:T(4,128)S(1)}, f32[1,2,12,4,4,128]{5,4,3,2,1,0:T(4,128)S(1)}, u32[]{:S(2)}, u32[]{:S(2)}) collective-permute-start(f32[1,2,12,4,4,128]{5,4,3,2,1,0:T(4,128)S(1)} %pad_maximum_fusion.2), channel_id=1, source_target_pairs={{1,0},{2,1},{3,2},{4,3},{5,4},{6,5},{7,6},{9,8},{10,9},{11,10},{12... | collective-permute-start | bytes 589832 | tf_op jit(solution)/shard_map/ppermute | solution.py:19
  185.1 11.6 %collective-permute-start.6 = (f32[1,2,12,4,4,128]{5,4,3,2,1,0:T(4,128)S(1)}, f32[1,2,12,4,4,128]{5,4,3,2,1,0:T(4,128)S(1)}, u32[]{:S(2)}, u32[]{:S(2)}) collective-permute-start(f32[1,2,12,4,4,128]{5,4,3,2,1,0:T(4,128)S(1)} %pad_maximum_fusion.2), channel_id=1, source_target_pairs={{0,1},{1,2},{2,3},{3,4},{4,5},{5,6},{6,7},{8,9},{9,10},{10,11},{11... | collective-permute-start | bytes 589832 | tf_op jit(solution)/shard_map/ppermute | solution.py:17
  187.8 8.7 %collective-permute-start.11 = (f32[2,4,4,128]{3,2,0,1:T(4,128)S(1)}, f32[2,4,4,128]{3,2,0,1:T(4,128)S(1)}, u32[]{:S(2)}, u32[]{:S(2)}) collective-permute-start(f32[2,4,4,128]{3,2,0,1:T(4,128)S(1)} %slice_bitcast_fusion.46), channel_id=1, source_target_pairs={{1,0},{2,1},{3,2},{4,3},{5,4},{6,5},{7,6},{9,8},{10,9},{11,10},{12... | collective-permute-start | bytes 49160 | tf_op jit(solution)/shard_map/ppermute | solution.py:29
  190.7 11.1 %collective-permute-start.15 = (f32[1,2,12,4,4,128]{5,4,3,2,1,0:T(4,128)S(1)}, f32[1,2,12,4,4,128]{5,4,3,2,1,0:T(4,128)S(1)}, u32[]{:S(2)}, u32[]{:S(2)}) collective-permute-start(f32[1,2,12,4,4,128]{5,4,3,2,1,0:T(4,128)S(1)} %pad_maximum_fusion.3), channel_id=1, source_target_pairs={{1,0},{2,1},{3,2},{4,3},{5,4},{6,5},{7,6},{9,8},{10,9},{11,10},{12... | collective-permute-start | bytes 589832 | tf_op jit(solution)/shard_map/ppermute | solution.py:19
  192.6 9.2 %collective-permute-start.14 = (f32[1,2,12,4,4,128]{5,4,3,2,1,0:T(4,128)S(1)}, f32[1,2,12,4,4,128]{5,4,3,2,1,0:T(4,128)S(1)}, u32[]{:S(2)}, u32[]{:S(2)}) collective-permute-start(f32[1,2,12,4,4,128]{5,4,3,2,1,0:T(4,128)S(1)} %pad_maximum_fusion.3), channel_id=1, source_target_pairs={{0,1},{1,2},{2,3},{3,4},{4,5},{5,6},{6,7},{8,9},{9,10},{10,11},{11... | collective-permute-start | bytes 589832 | tf_op jit(solution)/shard_map/ppermute | solution.py:17
  207.6 157.0 %copy-start.2 = (f32[256,512]{0,1:T(8,128)S(1)}, f32[256,512]{0,1:T(8,128)}, u32[]{:S(2)}) copy-start(f32[256,512]{0,1:T(8,128)} %get-tuple-element.434) | copy-start | bytes 1572868
  207.7 157.0 %copy-start.3 = (f32[256,512]{0,1:T(8,128)S(1)}, f32[256,512]{0,1:T(8,128)}, u32[]{:S(2)}) copy-start(f32[256,512]{0,1:T(8,128)} %get-tuple-element.435) | copy-start | bytes 1572868
  211.1 156.7 %copy-start.127 = (f32[4,4,256]{2,1,0:T(4,128)S(1)}, f32[4,4,256]{2,1,0:T(4,128)}, u32[]{:S(2)}) copy-start(f32[4,4,256]{2,1,0:T(4,128)} %copy-done.126) | copy-start | bytes 49156
  211.1 156.7 %copy-start.129 = (f32[4,4,256]{2,1,0:T(4,128)S(1)}, f32[4,4,256]{2,1,0:T(4,128)}, u32[]{:S(2)}) copy-start(f32[4,4,256]{2,1,0:T(4,128)} %copy-done.128) | copy-start | bytes 49156
  211.2 157.1 %copy-start.11 = (bf16[2,128,128]{2,1,0:T(8,128)(2,1)S(1)}, bf16[2,128,128]{2,1,0:T(8,128)(2,1)}, u32[]{:S(2)}) copy-start(bf16[2,128,128]{2,1,0:T(8,128)(2,1)} %param.43) | copy-start | bytes 196612
  (109 other events, 1101.1 us)
Sparse Core Ops, SparseCore 0:
  17.9 175.8 all-gather.4
  198.5 166.0 all-gather.2
where the time goes:
time: 381 us; the launch traced here: 378 us
  waiting for transfers between devices  156 us (41%)
  local copies, waits for them, and re-layouts  93.3 us (24%)
  starting transfers between devices  48.6 us (13%)
  other arithmetic  47.6 us (12%)
  matrix products  16.4 us (4%)
  between operations  16.4 us (4%)
    all_gather x2, waiting for transfers between devices, far_field(): lax.all_gather(top_b[:, :, None], ('row', 'col'), axis=2, tiled=True)  153 us
    unnamed x333, local copies, waits for them, and re-layouts  52.9 us
    ppermute x6, starting transfers between devices, with_halo(): lax.ppermute(tail, axis, [(i, (i + 1) % count) for i in range(ends)])  23.6 us
    ppermute x6, starting transfers between devices, with_halo(): lax.ppermute(head, axis, [((i + 1) % count, i) for i in range(ends)])  17.5 us
    dot_general x25, matrix products, product(): return jnp.einsum(form, left, right, preferred_element_type=jnp.float32)  14.3 us
    slice x3, local copies, waits for them, and re-layouts, conj_flip(): return jnp.stack([flipped[0], -flipped[1]])  11.5 us
    gather x2, local copies, waits for them, and re-layouts, far_field(): coeff = jnp.take(flat_tab, flat_index, axis=2).astype(jnp.float32)  8.56 us
  transfers between devices with their start and end apart: 18, of which 2 were waited for; matrix products, arithmetic and copies ran while one was open for 37% of the time, Pallas kernels for 0%

commit v1 on v0

--- a/solution.py
+++ b/solution.py
@@ -135,7 +135,19 @@
     flat_tab = coarse_tab.reshape(
         coarse_tab.shape[0], 2, coarse_tab.shape[2] * coarse_tab.shape[3], coarse_tab.shape[4]
     )
-    portion = lax.all_gather(top_b[:, :, None], ("row", "col"), axis=2, tiled=True)
+
+    def connect_heaps(block_in):
+        return jnp.concatenate(
+            jax.lax.all_to_all(
+                jnp.stack([block_in] * jax.lax.axis_size(("row", "col")), axis=0),
+                ("row", "col"),
+                0,
+                0,
+            ),
+            axis=2,
+        )
+
+    portion = connect_heaps(top_b[:, :, None])
     sources = jnp.arange(portion.shape[2])
     src_rows = sources // col_count
     src_cols = sources % col_count

time: 381 us -> 313 us (0.82)
  waiting for transfers between devices: 156 us -> 71.8 us
  starting transfers between devices: 48.6 us -> 96.5 us
  local copies, waits for them, and re-layouts: 93.3 us -> 78.8 us
  between operations: 16.4 us -> 3.08 us
  other arithmetic: 47.6 us -> 41.9 us
    all_gather x2 -> x0, waiting for transfers between devices: 153 us -> none  [far_field(): lax.all_gather(top_b[:, :, None], ('row', 'col'), axis=2, tiled=True)]
    all_to_all x0 -> x2, waiting for transfers between devices: none -> 69.5 us  [connect_heaps(): jax.lax.all_to_all(jnp.stack([block_in] * jax.lax.axis_size(('row', 'col'...]
    all_to_all x0 -> x2, starting transfers between devices: none -> 47.5 us  [connect_heaps(): jax.lax.all_to_all(jnp.stack([block_in] * jax.lax.axis_size(('row', 'col'...]
    unnamed x333 -> x239, local copies, waits for them, and re-layouts: 52.9 us -> 38.2 us
  transfers between devices with their start and end apart: 18 -> 18, of which waited for: 2 -> 2; matrix products, arithmetic and copies ran while one was open for 37% -> 41% of each run, Pallas kernels for 0% -> 0%
where the time goes in v1:
time: 313 us; the launch traced here: 307 us
  starting transfers between devices  96.5 us (31%)
  local copies, waits for them, and re-layouts  78.8 us (25%)
  waiting for transfers between devices  71.8 us (23%)
  other arithmetic  41.9 us (13%)
  matrix products  14.9 us (5%)
    all_to_all x2, waiting for transfers between devices, connect_heaps(): jax.lax.all_to_all(jnp.stack([block_in] * jax.lax.axis_size(('row', 'col'...  69.5 us
    all_to_all x2, starting transfers between devices, connect_heaps(): jax.lax.all_to_all(jnp.stack([block_in] * jax.lax.axis_size(('row', 'col'...  47.5 us
    unnamed x239, local copies, waits for them, and re-layouts  38.2 us
    ppermute x6, starting transfers between devices, with_halo(): lax.ppermute(tail, axis, [(i, (i + 1) % count) for i in range(ends)])  22 us
    ppermute x6, starting transfers between devices, with_halo(): lax.ppermute(head, axis, [((i + 1) % count, i) for i in range(ends)])  18.7 us
    dot_general x25, matrix products, product(): return jnp.einsum(form, left, right, preferred_element_type=jnp.float32)  12.8 us
    slice x3, local copies, waits for them, and re-layouts, conj_flip(): return jnp.stack([flipped[0], -flipped[1]])  11.4 us
    ppermute x4, starting transfers between devices, from_behind(): return lax.ppermute(block, axis, route)  8.35 us
  transfers between devices with their start and end apart: 18, of which 2 were waited for; matrix products, arithmetic and copies ran while one was open for 41% of the time, Pallas kernels for 0%

profile of v1, /device:TPU:1, one launch (start us, length us, event | category | flops | bytes accessed | tf_op | source)
XLA Modules:
  0.0 307.0 jit_solution(17444984956518834403)
XLA Ops:
  5.0 1.3 collective-permute-start.5
  6.3 5.6 %collective-permute-start.4 = (f32[1,2,4,4,4,128]{5,4,3,2,1,0:T(4,128)}, f32[1,2,4,4,4,128]{5,4,3,2,1,0:T(4,128)}, u32[]{:S(2)}, u32[]{:S(2)}) collective-permute-start(f32[1,2,4,4,4,128]{5,4,3,2,1,0:T(4,128)} %pad_maximum_fusion.5), channel_id=1, source_target_pairs={{0,8},{8,16},{16,24},{24,32},{32,40},{40,48},{48,56},{56,64},{64,7... | collective-permute-start | bytes 196616 | tf_op jit(solution)/shard_map/ppermute | solution.py:17
  11.9 1.3 fusion.136
  13.2 1.3 collective-permute-start.1
  14.5 4.0 %collective-permute-start = (bf16[2,1,4,4,128]{4,3,2,1,0:T(4,128)(2,1)}, bf16[2,1,4,4,128]{4,3,2,1,0:T(4,128)(2,1)S(1)}, u32[]{:S(2)}, u32[]{:S(2)}) collective-permute-start(bf16[2,1,4,4,128]{4,3,2,1,0:T(4,128)(2,1)} %get-tuple-element.431), channel_id=1, source_target_pairs={{0,8},{8,16},{16,24},{24,32},{32,40},{40,48},{48,56},{56,64},{64,7... | collective-permute-start | bytes 24584 | tf_op jit(solution)/shard_map/ppermute | solution.py:17
  25.3 1.8 stack.775
  27.1 27.0 %all-to-all-start.1 = ((bf16[512,1,2,1,4,256]{5,4,3,2,1,0:T(4,128)(2,1)}), bf16[512,1,2,1,4,256]{5,4,3,2,1,0:T(4,128)(2,1)}, u32[]{:S(2)}, u32[]{:S(2)}) async-start(bf16[512,1,2,1,4,256]{5,4,3,2,1,0:T(4,128)(2,1)} %stack.775), calls=%async_computation.1 | async-start | bytes 4194304 | tf_op jit(solution)/shard_map/all_to_all | solution.py:141
  54.7 1.7 collective-permute-start.13
  57.8 6.3 %fusion.125 = (bf16[1,127,15,256]{3,0,2,1:T(2,128)(2,1)}, bf16[1,127,15,256]{3,0,2,1:T(2,128)(2,1)S(1)}) fusion(bf16[2,127,15,256]{3,0,2,1:T(2,128)(2,1)} %param.47), kind=kLoop, calls=%fused_computation.445 | loop fusion | bytes 3901440 | tf_op jit(solution)/shard_map/slice | solution.py:38
  64.1 3.3 %reverse_negate_fusion = bf16[1,127,15,256]{3,0,2,1:T(2,128)(2,1)} fusion(bf16[1,127,15,256]{3,0,2,1:T(2,128)(2,1)S(1)} %get-tuple-element.296), kind=kLoop, calls=%fused_computation.19 | loop fusion | flops 1463040 | bytes 1950720 | tf_op jit(solution)/shard_map/neg | solution.py:38
  67.4 4.9 %slice.1246 = bf16[1,127,15,256]{3,0,2,1:T(2,128)(2,1)} reverse(bf16[1,127,15,256]{3,0,2,1:T(2,128)(2,1)} %get-tuple-element.295), dimensions={1,2} | reverse | bytes 1950720 | tf_op jit(solution)/shard_map/slice | solution.py:38
  72.9 1.8 fusion.131
  77.8 1.4 and_reduce_fusion
  79.2 1.2 add_dynamic-update-slice_fusion
  80.4 1.9 fusion.63
  84.7 6.7 %maximum_bitcast_fusion = bf16[2,1905,256]{2,0,1:T(2,128)(2,1)} fusion(bf16[1,1,1905,256]{3,1,2,0:T(2,128)(2,1)} %bitcast.1065, bf16[1,1,1905,256]{3,1,2,0:T(2,128)(2,1)} %bitcast.1066), kind=kLoop, calls=%fused_computation.18 | loop fusion | flops 3901440 | bytes 3901440 | tf_op jit(solution)/shard_map/jit(_take)/Arg_0.13 | solution.py:157
  93.2 4.3 %gather_fusion.1 = bf16[512,2,256]{2,1,0:T(2,128)(2,1)} fusion(bf16[2,1905,256]{2,0,1:T(2,128)(2,1)} %maximum_bitcast_fusion, s32[1024]{0:T(1024)S(1)} %pad_clamp_fusion), kind=kCustom, calls=%fused_computation.1.clone | custom fusion | bytes 1050624 | tf_op jit(solution)/shard_map/jit(_take)/gather | solution.py:157
  97.4 3.6 %gather_fusion = bf16[512,2,256]{2,1,0:T(2,128)(2,1)S(1)} fusion(bf16[2,1905,256]{2,0,1:T(2,128)(2,1)} %bitcast.1063, s32[1024]{0:T(1024)} %copy-done.84), kind=kCustom, calls=%fused_computation.clone | custom fusion | bytes 1050624 | tf_op jit(solution)/shard_map/jit(_take)/gather | solution.py:157
  101.1 1.5 copy.425
  102.6 1.7 copy_bitcast_fusion.43
  104.3 1.6 copy_bitcast_fusion.41
  105.9 1.6 copy_bitcast_fusion.33
  117.9 1.8 fusion.45
  120.6 1.4 fusion.49
  122.1 6.3 %collective-permute-start.3 = (bf16[2,6,1,4,128]{4,3,2,1,0:T(4,128)(2,1)S(1)}, bf16[2,6,1,4,128]{4,3,2,1,0:T(4,128)(2,1)S(1)}, u32[]{:S(2)}, u32[]{:S(2)}) collective-permute-start(bf16[2,6,1,4,128]{4,3,2,1,0:T(4,128)(2,1)S(1)} %get-tuple-element.419), channel_id=1, source_target_pairs={{1,0},{2,1},{3,2},{4,3},{5,4},{6,5},{7,6},{9,8},{10,9},{11,10},{12... | collective-permute-start | bytes 36872 | tf_op jit(solution)/shard_map/ppermute | solution.py:19
  128.4 1.9 collective-permute-start.2
  151.0 4.9 %collective-permute-start.12 = (f32[1,2,4,4,4,128]{5,4,3,2,1,0:T(4,128)}, f32[1,2,4,4,4,128]{5,4,3,2,1,0:T(4,128)}, u32[]{:S(2)}, u32[]{:S(2)}) collective-permute-start(f32[1,2,4,4,4,128]{5,4,3,2,1,0:T(4,128)} %pad_maximum_fusion.6), channel_id=1, source_target_pairs={{0,8},{8,16},{16,24},{24,32},{32,40},{40,48},{48,56},{56,64},{64,7... | collective-permute-start | bytes 196616 | tf_op jit(solution)/shard_map/ppermute | solution.py:17
  155.9 1.9 collective-permute-start.8
  161.4 3.8 %stack.599 = bf16[9,2,4,4,4,128]{5,0,4,1,3,2:T(8,128)(2,1)} concatenate(bf16[1,2,4,4,4,128]{5,0,4,1,3,2:T(2,128)(2,1)S(1)} %copy.249, bf16[1,2,4,4,4,128]{5,0,4,1,3,2:T(2,128)(2,1)S(1)} %copy.250, bf16[1,2,4,4,4,128]{5,0,4,1,3,2:T(2,128)(2,1)} %copy.251, bf16[1,2,4,4,4,128]{5,0,4,1,3,2:T(2,128)(2,1)} %copy.252, bf16[1,2,4,4,4,128]{5,0,4,1,3,2:T(2,128)(2,1)S(1)} %copy.253, ...), dimensions={0} | concatenate | bytes 589824 | tf_op jit(solution)/shard_map/stack | solution.py:51
  165.1 1.3 fusion.10
  168.4 1.3 collective-permute-start.9
  170.8 2.3 collective-permute-done.9
  173.0 2.7 collective-permute-start.10
  175.8 1.8 stack.682
  177.6 20.5 %all-to-all-start = ((bf16[512,1,2,1,4,256]{5,4,3,2,1,0:T(4,128)(2,1)}), bf16[512,1,2,1,4,256]{5,4,3,2,1,0:T(4,128)(2,1)S(1)}, u32[]{:S(2)}, u32[]{:S(2)}) async-start(bf16[512,1,2,1,4,256]{5,4,3,2,1,0:T(4,128)(2,1)} %stack.682), calls=%async_computation | async-start | bytes 4194304 | tf_op jit(solution)/shard_map/all_to_all | solution.py:141
  199.5 6.2 %collective-permute-start.7 = (f32[1,2,12,4,4,128]{5,4,3,2,1,0:T(4,128)S(1)}, f32[1,2,12,4,4,128]{5,4,3,2,1,0:T(4,128)S(1)}, u32[]{:S(2)}, u32[]{:S(2)}) collective-permute-start(f32[1,2,12,4,4,128]{5,4,3,2,1,0:T(4,128)S(1)} %pad_maximum_fusion.2), channel_id=1, source_target_pairs={{1,0},{2,1},{3,2},{4,3},{5,4},{6,5},{7,6},{9,8},{10,9},{11,10},{12... | collective-permute-start | bytes 589832 | tf_op jit(solution)/shard_map/ppermute | solution.py:19
  205.7 1.9 collective-permute-start.6
  207.7 2.4 collective-permute-start.11
  211.0 1.9 collective-permute-start.15
  213.0 3.6 %collective-permute-start.14 = (f32[1,2,12,4,4,128]{5,4,3,2,1,0:T(4,128)S(1)}, f32[1,2,12,4,4,128]{5,4,3,2,1,0:T(4,128)S(1)}, u32[]{:S(2)}, u32[]{:S(2)}) collective-permute-start(f32[1,2,12,4,4,128]{5,4,3,2,1,0:T(4,128)S(1)} %pad_maximum_fusion.3), channel_id=1, source_target_pairs={{0,1},{1,2},{2,3},{3,4},{4,5},{5,6},{6,7},{8,9},{9,10},{10,11},{11... | collective-permute-start | bytes 589832 | tf_op jit(solution)/shard_map/ppermute | solution.py:17
  216.8 1.2 pad_maximum_fusion
  220.5 1.2 subtract_reduce_fusion.31
  221.9 1.2 pad_maximum_fusion.1
  223.2 1.8 subtract_reduce_fusion.6
  226.5 1.2 subtract_reduce_fusion.15
  227.9 3.1 %fusion.6 = (f32[256,4]{0,1:T(4,128)S(1)}, f32[256,4]{0,1:T(4,128)S(1)}, f32[256,4]{0,1:T(4,128)S(1)}, f32[256,4]{0,1:T(4,128)S(1)}) fusion(f32[256,512]{0,1:T(8,128)S(1)} %copy-done.4, bf16[1,2,512,4,256]{4,3,1,2,0:T(4,128)(2,1)} %bitcast.281, f32[256,512]{0,1:T(8,128)S(1)} %copy-done.3), kind=kLoop, calls=%fused_computation.16 | loop fusion | flops 5238784 | bytes 3162112 | tf_op jit(solution)/shard_map/snq,snmq->smq/dot_general | solution.py:164
  231.0 69.5 %all-to-all-done = bf16[512,1,2,1,4,256]{5,4,3,2,1,0:T(4,128)(2,1)S(1)} async-done(((bf16[512,1,2,1,4,256]{5,4,3,2,1,0:T(4,128)(2,1)}), bf16[512,1,2,1,4,256]{5,4,3,2,1,0:T(4,128)(2,1)S(1)}, u32[]{:S(2)}, u32[]{:S(2)}) %all-to-all-start) | async-done | bytes 2097184 | tf_op jit(solution)/shard_map/all_to_all | solution.py:141
  300.6 3.0 fusion.2
  (395 shorter events, 68.0 us)
Async XLA Ops:
  0.6 23.3 %copy-start = (f32[256,128]{1,0:T(8,128)S(1)}, f32[256,128]{1,0:T(8,128)}, u32[]{:S(2)}) copy-start(f32[256,128]{1,0:T(8,128)} %param.44) | copy-start | bytes 393220
  5.0 193.3 %collective-permute-start.5 = (f32[1,2,4,4,4,128]{5,4,3,2,1,0:T(4,128)}, f32[1,2,4,4,4,128]{5,4,3,2,1,0:T(4,128)}, u32[]{:S(2)}, u32[]{:S(2)}) collective-permute-start(f32[1,2,4,4,4,128]{5,4,3,2,1,0:T(4,128)} %pad_maximum_fusion.5), channel_id=1, source_target_pairs={{8,0},{16,8},{24,16},{32,24},{40,32},{48,40},{56,48},{64,56},{72,6... | collective-permute-start | bytes 196616 | tf_op jit(solution)/shard_map/ppermute | solution.py:19
  6.3 192.0 %collective-permute-start.4 = (f32[1,2,4,4,4,128]{5,4,3,2,1,0:T(4,128)}, f32[1,2,4,4,4,128]{5,4,3,2,1,0:T(4,128)}, u32[]{:S(2)}, u32[]{:S(2)}) collective-permute-start(f32[1,2,4,4,4,128]{5,4,3,2,1,0:T(4,128)} %pad_maximum_fusion.5), channel_id=1, source_target_pairs={{0,8},{8,16},{16,24},{24,32},{32,40},{40,48},{48,56},{56,64},{64,7... | collective-permute-start | bytes 196616 | tf_op jit(solution)/shard_map/ppermute | solution.py:17
  13.2 108.7 %collective-permute-start.1 = (bf16[2,1,4,4,128]{4,3,2,1,0:T(4,128)(2,1)}, bf16[2,1,4,4,128]{4,3,2,1,0:T(4,128)(2,1)S(1)}, u32[]{:S(2)}, u32[]{:S(2)}) collective-permute-start(bf16[2,1,4,4,128]{4,3,2,1,0:T(4,128)(2,1)} %get-tuple-element.430), channel_id=1, source_target_pairs={{8,0},{16,8},{24,16},{32,24},{40,32},{48,40},{56,48},{64,56},{72,6... | collective-permute-start | bytes 24584 | tf_op jit(solution)/shard_map/ppermute | solution.py:19
  14.5 107.4 %collective-permute-start = (bf16[2,1,4,4,128]{4,3,2,1,0:T(4,128)(2,1)}, bf16[2,1,4,4,128]{4,3,2,1,0:T(4,128)(2,1)S(1)}, u32[]{:S(2)}, u32[]{:S(2)}) collective-permute-start(bf16[2,1,4,4,128]{4,3,2,1,0:T(4,128)(2,1)} %get-tuple-element.431), channel_id=1, source_target_pairs={{0,8},{8,16},{16,24},{24,32},{32,40},{40,48},{48,56},{56,64},{64,7... | collective-permute-start | bytes 24584 | tf_op jit(solution)/shard_map/ppermute | solution.py:17
  27.1 29.4 %copy-start.1 = (bf16[2,4,4,2,128,128]{5,4,3,2,1,0:T(8,128)(2,1)S(1)}, bf16[2,4,4,2,128,128]{5,4,3,2,1,0:T(8,128)(2,1)}, u32[]{:S(2)}) copy-start(bf16[2,4,4,2,128,128]{5,4,3,2,1,0:T(8,128)(2,1)} %param.41) | copy-start | bytes 6291460
  27.1 29.4 %copy-start.9 = (bf16[2,4,4,4,128]{4,3,2,1,0:T(4,128)(2,1)S(1)}, bf16[2,4,4,4,128]{4,3,2,1,0:T(4,128)(2,1)}, u32[]{:S(2)}) copy-start(bf16[2,4,4,4,128]{4,3,2,1,0:T(4,128)(2,1)} %param.39) | copy-start | bytes 98308
  27.1 148.7 %all-to-all-start.1 = ((bf16[512,1,2,1,4,256]{5,4,3,2,1,0:T(4,128)(2,1)}), bf16[512,1,2,1,4,256]{5,4,3,2,1,0:T(4,128)(2,1)}, u32[]{:S(2)}, u32[]{:S(2)}) async-start(bf16[512,1,2,1,4,256]{5,4,3,2,1,0:T(4,128)(2,1)} %stack.775), calls=%async_computation.1 | async-start | bytes 4194304 | tf_op jit(solution)/shard_map/all_to_all | solution.py:141
  54.7 155.4 %collective-permute-start.13 = (f32[1,2,4,4,4,128]{5,4,3,2,1,0:T(4,128)}, f32[1,2,4,4,4,128]{5,4,3,2,1,0:T(4,128)}, u32[]{:S(2)}, u32[]{:S(2)}) collective-permute-start(f32[1,2,4,4,4,128]{5,4,3,2,1,0:T(4,128)} %pad_maximum_fusion.6), channel_id=1, source_target_pairs={{8,0},{16,8},{24,16},{32,24},{40,32},{48,40},{56,48},{64,56},{72,6... | collective-permute-start | bytes 196616 | tf_op jit(solution)/shard_map/ppermute | solution.py:19
  57.0 20.1 %copy-start.89 = (s32[2]{0:T(128)}, s32[2]{0:T(128)S(1)}, u32[]{:S(2)}) copy-start(s32[2]{0:T(128)S(1)} %iota_multiply_fusion) | copy-start | bytes 28
  72.3 20.9 %copy-start.84 = (s32[1024]{0:T(1024)}, s32[1024]{0:T(1024)S(1)}, u32[]{:S(2)}) copy-start(s32[1024]{0:T(1024)S(1)} %pad_clamp_fusion) | copy-start | bytes 12292
  102.6 8.3 %copy-start.73 = (f32[1,1,12,12,128]{4,1,3,2,0:T(1,128)S(1)}, f32[1,1,12,12,128]{4,1,3,2,0:T(1,128)}, u32[]{:S(2)}) copy-start(f32[1,1,12,12,128]{4,1,3,2,0:T(1,128)} %get-tuple-element.377) | copy-start | bytes 221188
  102.6 8.3 %copy-start.74 = (f32[1,1,12,12,128]{4,1,3,2,0:T(1,128)S(1)}, f32[1,1,12,12,128]{4,1,3,2,0:T(1,128)}, u32[]{:S(2)}) copy-start(f32[1,1,12,12,128]{4,1,3,2,0:T(1,128)} %get-tuple-element.378) | copy-start | bytes 221188
  120.5 9.8 %copy-start.86 = (bf16[4,256]{1,0:T(4,128)(2,1)S(1)}, bf16[4,256]{1,0:T(4,128)(2,1)}, u32[]{:S(2)}) copy-start(bf16[4,256]{1,0:T(4,128)(2,1)} %get-tuple-element.293) | copy-start | bytes 6148
  120.5 9.8 %copy-start.87 = (bf16[4,256]{1,0:T(4,128)(2,1)S(1)}, bf16[4,256]{1,0:T(4,128)(2,1)}, u32[]{:S(2)}) copy-start(bf16[4,256]{1,0:T(4,128)(2,1)} %get-tuple-element.294) | copy-start | bytes 6148
  122.1 29.0 %collective-permute-start.3 = (bf16[2,6,1,4,128]{4,3,2,1,0:T(4,128)(2,1)S(1)}, bf16[2,6,1,4,128]{4,3,2,1,0:T(4,128)(2,1)S(1)}, u32[]{:S(2)}, u32[]{:S(2)}) collective-permute-start(bf16[2,6,1,4,128]{4,3,2,1,0:T(4,128)(2,1)S(1)} %get-tuple-element.419), channel_id=1, source_target_pairs={{1,0},{2,1},{3,2},{4,3},{5,4},{6,5},{7,6},{9,8},{10,9},{11,10},{12... | collective-permute-start | bytes 36872 | tf_op jit(solution)/shard_map/ppermute | solution.py:19
  128.4 27.6 %collective-permute-start.2 = (bf16[2,6,1,4,128]{4,3,2,1,0:T(4,128)(2,1)S(1)}, bf16[2,6,1,4,128]{4,3,2,1,0:T(4,128)(2,1)S(1)}, u32[]{:S(2)}, u32[]{:S(2)}) collective-permute-start(bf16[2,6,1,4,128]{4,3,2,1,0:T(4,128)(2,1)S(1)} %get-tuple-element.420), channel_id=1, source_target_pairs={{0,1},{1,2},{2,3},{3,4},{4,5},{5,6},{6,7},{8,9},{9,10},{10,11},{11... | collective-permute-start | bytes 36872 | tf_op jit(solution)/shard_map/ppermute | solution.py:17
  151.0 59.1 %collective-permute-start.12 = (f32[1,2,4,4,4,128]{5,4,3,2,1,0:T(4,128)}, f32[1,2,4,4,4,128]{5,4,3,2,1,0:T(4,128)}, u32[]{:S(2)}, u32[]{:S(2)}) collective-permute-start(f32[1,2,4,4,4,128]{5,4,3,2,1,0:T(4,128)} %pad_maximum_fusion.6), channel_id=1, source_target_pairs={{0,8},{8,16},{16,24},{24,32},{32,40},{40,48},{48,56},{56,64},{64,7... | collective-permute-start | bytes 196616 | tf_op jit(solution)/shard_map/ppermute | solution.py:17
  155.9 11.7 %collective-permute-start.8 = (f32[2,6,4,128]{3,2,0,1:T(4,128)}, f32[2,6,4,128]{3,2,0,1:T(4,128)}, u32[]{:S(2)}, u32[]{:S(2)}) collective-permute-start(f32[2,6,4,128]{3,2,0,1:T(4,128)} %slice_bitcast_fusion.41), channel_id=1, source_target_pairs={{0,8},{8,16},{16,24},{24,32},{32,40},{40,48},{48,56},{56,64},{64,7... | collective-permute-start | bytes 73736 | tf_op jit(solution)/shard_map/ppermute | solution.py:29
  168.4 4.6 %collective-permute-start.9 = (f32[2,6,4,128]{3,2,0,1:T(4,128)S(1)}, f32[2,6,4,128]{3,2,0,1:T(4,128)S(1)}, u32[]{:S(2)}, u32[]{:S(2)}) collective-permute-start(f32[2,6,4,128]{3,2,0,1:T(4,128)S(1)} %slice_bitcast_fusion.40), channel_id=1, source_target_pairs={{8,0},{16,8},{24,16},{32,24},{40,32},{48,40},{56,48},{64,56},{72,6... | collective-permute-start | bytes 73736 | tf_op jit(solution)/shard_map/ppermute | solution.py:29
  173.0 34.6 %collective-permute-start.10 = (f32[2,4,4,128]{3,2,0,1:T(4,128)S(1)}, f32[2,4,4,128]{3,2,0,1:T(4,128)S(1)}, u32[]{:S(2)}, u32[]{:S(2)}) collective-permute-start(f32[2,4,4,128]{3,2,0,1:T(4,128)S(1)} %slice_bitcast_fusion.47), channel_id=1, source_target_pairs={{0,1},{1,2},{2,3},{3,4},{4,5},{5,6},{6,7},{8,9},{9,10},{10,11},{11... | collective-permute-start | bytes 49160 | tf_op jit(solution)/shard_map/ppermute | solution.py:29
  177.6 122.9 %all-to-all-start = ((bf16[512,1,2,1,4,256]{5,4,3,2,1,0:T(4,128)(2,1)}), bf16[512,1,2,1,4,256]{5,4,3,2,1,0:T(4,128)(2,1)S(1)}, u32[]{:S(2)}, u32[]{:S(2)}) async-start(bf16[512,1,2,1,4,256]{5,4,3,2,1,0:T(4,128)(2,1)} %stack.682), calls=%async_computation | async-start | bytes 4194304 | tf_op jit(solution)/shard_map/all_to_all | solution.py:141
  198.1 19.9 %copy-start.57 = (f32[12,12,128]{2,1,0:T(8,128)S(1)}, f32[12,12,128]{2,1,0:T(8,128)}, u32[]{:S(2)}) copy-start(f32[12,12,128]{2,1,0:T(8,128)} %get-tuple-element.454) | copy-start | bytes 221188
  198.1 19.9 %copy-start.58 = (f32[12,12,128]{2,1,0:T(8,128)S(1)}, f32[12,12,128]{2,1,0:T(8,128)}, u32[]{:S(2)}) copy-start(f32[12,12,128]{2,1,0:T(8,128)} %get-tuple-element.455) | copy-start | bytes 221188
  198.1 19.9 %copy-start.59 = (f32[12,12,128]{2,1,0:T(8,128)S(1)}, f32[12,12,128]{2,1,0:T(8,128)}, u32[]{:S(2)}) copy-start(f32[12,12,128]{2,1,0:T(8,128)} %get-tuple-element.452) | copy-start | bytes 221188
  198.2 19.9 %copy-start.60 = (f32[12,12,128]{2,1,0:T(8,128)S(1)}, f32[12,12,128]{2,1,0:T(8,128)}, u32[]{:S(2)}) copy-start(f32[12,12,128]{2,1,0:T(8,128)} %get-tuple-element.453) | copy-start | bytes 221188
  198.2 19.9 %copy-start.61 = (f32[12,12,128]{2,1,0:T(8,128)S(1)}, f32[12,12,128]{2,1,0:T(8,128)}, u32[]{:S(2)}) copy-start(f32[12,12,128]{2,1,0:T(8,128)} %get-tuple-element.450) | copy-start | bytes 221188
  198.2 19.9 %copy-start.62 = (f32[12,12,128]{2,1,0:T(8,128)S(1)}, f32[12,12,128]{2,1,0:T(8,128)}, u32[]{:S(2)}) copy-start(f32[12,12,128]{2,1,0:T(8,128)} %get-tuple-element.451) | copy-start | bytes 221188
  198.2 19.9 %copy-start.63 = (f32[12,12,128]{2,1,0:T(8,128)S(1)}, f32[12,12,128]{2,1,0:T(8,128)}, u32[]{:S(2)}) copy-start(f32[12,12,128]{2,1,0:T(8,128)} %get-tuple-element.442) | copy-start | bytes 221188
  198.2 19.9 %copy-start.64 = (f32[12,12,128]{2,1,0:T(8,128)S(1)}, f32[12,12,128]{2,1,0:T(8,128)}, u32[]{:S(2)}) copy-start(f32[12,12,128]{2,1,0:T(8,128)} %get-tuple-element.443) | copy-start | bytes 221188
  198.2 20.7 %copy-start.21 = (f32[12,12,128]{2,1,0:T(8,128)S(1)}, f32[12,12,128]{2,1,0:T(8,128)}, u32[]{:S(2)}) copy-start(f32[12,12,128]{2,1,0:T(8,128)} %get-tuple-element.460) | copy-start | bytes 221188
  198.2 20.7 %copy-start.22 = (f32[12,12,128]{2,1,0:T(8,128)S(1)}, f32[12,12,128]{2,1,0:T(8,128)}, u32[]{:S(2)}) copy-start(f32[12,12,128]{2,1,0:T(8,128)} %get-tuple-element.461) | copy-start | bytes 221188
  198.2 20.7 %copy-start.25 = (f32[12,12,128]{2,1,0:T(8,128)S(1)}, f32[12,12,128]{2,1,0:T(8,128)}, u32[]{:S(2)}) copy-start(f32[12,12,128]{2,1,0:T(8,128)} %get-tuple-element.458) | copy-start | bytes 221188
  198.2 20.7 %copy-start.26 = (f32[12,12,128]{2,1,0:T(8,128)S(1)}, f32[12,12,128]{2,1,0:T(8,128)}, u32[]{:S(2)}) copy-start(f32[12,12,128]{2,1,0:T(8,128)} %get-tuple-element.459) | copy-start | bytes 221188
  198.2 20.7 %copy-start.30 = (f32[12,12,128]{2,1,0:T(8,128)S(1)}, f32[12,12,128]{2,1,0:T(8,128)}, u32[]{:S(2)}) copy-start(f32[12,12,128]{2,1,0:T(8,128)} %get-tuple-element.456) | copy-start | bytes 221188
  198.3 20.7 %copy-start.31 = (f32[12,12,128]{2,1,0:T(8,128)S(1)}, f32[12,12,128]{2,1,0:T(8,128)}, u32[]{:S(2)}) copy-start(f32[12,12,128]{2,1,0:T(8,128)} %get-tuple-element.457) | copy-start | bytes 221188
  198.3 20.7 %copy-start.34 = (f32[12,12,128]{2,1,0:T(8,128)S(1)}, f32[12,12,128]{2,1,0:T(8,128)}, u32[]{:S(2)}) copy-start(f32[12,12,128]{2,1,0:T(8,128)} %get-tuple-element.444) | copy-start | bytes 221188
  198.3 20.7 %copy-start.35 = (f32[12,12,128]{2,1,0:T(8,128)S(1)}, f32[12,12,128]{2,1,0:T(8,128)}, u32[]{:S(2)}) copy-start(f32[12,12,128]{2,1,0:T(8,128)} %get-tuple-element.445) | copy-start | bytes 221188
  198.3 20.7 %copy-start.39 = (f32[12,12,128]{2,1,0:T(8,128)S(1)}, f32[12,12,128]{2,1,0:T(8,128)}, u32[]{:S(2)}) copy-start(f32[12,12,128]{2,1,0:T(8,128)} %get-tuple-element.446) | copy-start | bytes 221188
  198.3 20.7 %copy-start.40 = (f32[12,12,128]{2,1,0:T(8,128)S(1)}, f32[12,12,128]{2,1,0:T(8,128)}, u32[]{:S(2)}) copy-start(f32[12,12,128]{2,1,0:T(8,128)} %get-tuple-element.447) | copy-start | bytes 221188
  198.3 20.7 %copy-start.43 = (f32[12,12,128]{2,1,0:T(8,128)S(1)}, f32[12,12,128]{2,1,0:T(8,128)}, u32[]{:S(2)}) copy-start(f32[12,12,128]{2,1,0:T(8,128)} %get-tuple-element.448) | copy-start | bytes 221188
  198.3 20.7 %copy-start.44 = (f32[12,12,128]{2,1,0:T(8,128)S(1)}, f32[12,12,128]{2,1,0:T(8,128)}, u32[]{:S(2)}) copy-start(f32[12,12,128]{2,1,0:T(8,128)} %get-tuple-element.449) | copy-start | bytes 221188
  199.5 17.3 %collective-permute-start.7 = (f32[1,2,12,4,4,128]{5,4,3,2,1,0:T(4,128)S(1)}, f32[1,2,12,4,4,128]{5,4,3,2,1,0:T(4,128)S(1)}, u32[]{:S(2)}, u32[]{:S(2)}) collective-permute-start(f32[1,2,12,4,4,128]{5,4,3,2,1,0:T(4,128)S(1)} %pad_maximum_fusion.2), channel_id=1, source_target_pairs={{1,0},{2,1},{3,2},{4,3},{5,4},{6,5},{7,6},{9,8},{10,9},{11,10},{12... | collective-permute-start | bytes 589832 | tf_op jit(solution)/shard_map/ppermute | solution.py:19
  205.7 11.1 %collective-permute-start.6 = (f32[1,2,12,4,4,128]{5,4,3,2,1,0:T(4,128)S(1)}, f32[1,2,12,4,4,128]{5,4,3,2,1,0:T(4,128)S(1)}, u32[]{:S(2)}, u32[]{:S(2)}) collective-permute-start(f32[1,2,12,4,4,128]{5,4,3,2,1,0:T(4,128)S(1)} %pad_maximum_fusion.2), channel_id=1, source_target_pairs={{0,1},{1,2},{2,3},{3,4},{4,5},{5,6},{6,7},{8,9},{9,10},{10,11},{11... | collective-permute-start | bytes 589832 | tf_op jit(solution)/shard_map/ppermute | solution.py:17
  207.7 9.0 %collective-permute-start.11 = (f32[2,4,4,128]{3,2,0,1:T(4,128)S(1)}, f32[2,4,4,128]{3,2,0,1:T(4,128)S(1)}, u32[]{:S(2)}, u32[]{:S(2)}) collective-permute-start(f32[2,4,4,128]{3,2,0,1:T(4,128)S(1)} %slice_bitcast_fusion.46), channel_id=1, source_target_pairs={{1,0},{2,1},{3,2},{4,3},{5,4},{6,5},{7,6},{9,8},{10,9},{11,10},{12... | collective-permute-start | bytes 49160 | tf_op jit(solution)/shard_map/ppermute | solution.py:29
  211.0 10.8 %collective-permute-start.15 = (f32[1,2,12,4,4,128]{5,4,3,2,1,0:T(4,128)S(1)}, f32[1,2,12,4,4,128]{5,4,3,2,1,0:T(4,128)S(1)}, u32[]{:S(2)}, u32[]{:S(2)}) collective-permute-start(f32[1,2,12,4,4,128]{5,4,3,2,1,0:T(4,128)S(1)} %pad_maximum_fusion.3), channel_id=1, source_target_pairs={{1,0},{2,1},{3,2},{4,3},{5,4},{6,5},{7,6},{9,8},{10,9},{11,10},{12... | collective-permute-start | bytes 589832 | tf_op jit(solution)/shard_map/ppermute | solution.py:19
  213.0 8.9 %collective-permute-start.14 = (f32[1,2,12,4,4,128]{5,4,3,2,1,0:T(4,128)S(1)}, f32[1,2,12,4,4,128]{5,4,3,2,1,0:T(4,128)S(1)}, u32[]{:S(2)}, u32[]{:S(2)}) collective-permute-start(f32[1,2,12,4,4,128]{5,4,3,2,1,0:T(4,128)S(1)} %pad_maximum_fusion.3), channel_id=1, source_target_pairs={{0,1},{1,2},{2,3},{3,4},{4,5},{5,6},{6,7},{8,9},{9,10},{10,11},{11... | collective-permute-start | bytes 589832 | tf_op jit(solution)/shard_map/ppermute | solution.py:17
  231.0 72.9 %copy-start.8 = (bf16[2,128,128]{2,1,0:T(8,128)(2,1)S(1)}, bf16[2,128,128]{2,1,0:T(8,128)(2,1)}, u32[]{:S(2)}) copy-start(bf16[2,128,128]{2,1,0:T(8,128)(2,1)} %param.43) | copy-start | bytes 196612
  (62 other events, 261.5 us)
